TPU v7x, 128 devices: a whole 4x4x4 slice. The times are simulated.
128 devices in a mesh: seg: 8 (over x, core), leaf: 16 (over z, y).
Axes of the slice: x: 4, y: 4, z: 4, core: 2. Of those that a mesh axis runs over, the one named last changes fastest.
Arguments:
- queries: bfloat16 [32, 512, 5120], P('seg', 'leaf'), may hold values from -160 to 160
- leaf_keys: bfloat16 [32, 512, 1024], P('seg', 'leaf'), may hold values from -5 to 5
- leaf_values: bfloat16 [32, 512, 1024], P('seg', 'leaf'), may hold values from -6 to 6
- inner_keys: bfloat16 [16, 512, 1024], P('seg', 'leaf'), may hold values from -6 to 6
- inner_values: bfloat16 [16, 512, 1024], P('seg', 'leaf'), may hold values from -6 to 6
- out_grad: bfloat16 [32, 512, 5120], P('seg', 'leaf'), may hold values from -6 to 6
- ancestors: int32 [32, 4], replicated, may hold values from 0 to 15, as said below
- depths: int32 [32], replicated, may hold values from 3 to 4, as said below
Outputs:
- attention: bfloat16 [32, 512, 5120], P('seg', 'leaf')
- query_grad: bfloat16 [32, 512, 5120], P('seg', 'leaf')
- leaf_key_grad: bfloat16 [32, 512, 1024], P('seg', 'leaf')
- leaf_value_grad: bfloat16 [32, 512, 1024], P('seg', 'leaf')
- inner_key_grad: bfloat16 [16, 512, 1024], P('seg', 'leaf')
- inner_value_grad: bfloat16 [16, 512, 1024], P('seg', 'leaf')
Inputs may be any that keep to these rules, and one draw needn't show every extreme that they name: `ancestors`: leaves l and m with l // 4 == m // 4 have the same row. Entry k of a row is the leaf's ancestor at tree level k, entry 0 the prompt's segment; entries at or past the leaf's depth are 0. The live entries of one row have different values of i // 2. `depths`: equal within each aligned block of 4 leaves; some leaf has 4.
All inputs are finite; a program needn't handle non-finite values.
Results may differ from a plain program's by a relative error of at most 0.03.
Values may be sent and summed in bfloat16 or wider, within the bound.
No kernel may reach another device: no remote copies, remote signals or barrier semaphores. Data moves between devices by JAX's collectives and lax.ppermute only.
A program may use at most 128 MiB of HBM per device.

v0:
```python
import math
import jax
import jax.numpy as jnp
from jax import lax
from jax.sharding import PartitionSpec as P

HD = 128
NEG_FILL = -1e30


def head_major(packed, kv_heads, head_size):
    block_count, rows_here = (packed.shape[0], packed.shape[1])
    shaped = packed.reshape(block_count, rows_here, 2, kv_heads, head_size)
    return shaped.transpose(3, 0, 1, 2, 4).reshape(kv_heads, block_count, rows_here, 2 * head_size)


def column_major(stacked, kv_heads, head_size):
    block_count, rows_here = (stacked.shape[1], stacked.shape[2])
    shaped = stacked.reshape(kv_heads, block_count, rows_here, 2, head_size)
    return shaped.transpose(1, 2, 3, 0, 4).reshape(block_count, rows_here, 2 * kv_heads * head_size)


def attend_block(
    query_row_set,
    gradient_row_set,
    key_anc,
    value_anc,
    private_keys,
    private_values,
    anc_visible,
    own_visible,
):
    logit_scale = 1.0 / math.sqrt(query_row_set.shape[-1])
    score_anc = (
        jnp.einsum("bmd,ad->bma", query_row_set, key_anc, preferred_element_type=jnp.float32)
        * logit_scale
    )
    score_own = (
        jnp.einsum("flh,feh->fle", query_row_set, private_keys, preferred_element_type=jnp.float32)
        * logit_scale
    )
    score_anc = jnp.where(anc_visible[None, None, :], score_anc, NEG_FILL)
    score_own = jnp.where(own_visible[None], score_own, NEG_FILL)
    highest = jnp.maximum(
        jnp.max(score_anc, axis=-1, keepdims=True), jnp.max(score_own, axis=-1, keepdims=True)
    )
    weight_anc = jnp.exp(score_anc - highest)
    weight_own = jnp.exp(score_own - highest)
    denom_sum = jnp.sum(weight_anc, axis=-1, keepdims=True) + jnp.sum(
        weight_own, axis=-1, keepdims=True
    )
    prob_anc = weight_anc / denom_sum
    prob_own = weight_own / denom_sum
    round_anc = prob_anc.astype(jnp.bfloat16)
    private_round = prob_own.astype(jnp.bfloat16)
    attention_result = jnp.einsum(
        "bma,ad->bmd", round_anc, value_anc, preferred_element_type=jnp.float32
    ) + jnp.einsum(
        "oiz,ozv->oiv", private_round, private_values, preferred_element_type=jnp.float32
    )
    result_round = attention_result.astype(jnp.bfloat16)
    delta_rows = jnp.sum(
        gradient_row_set.astype(jnp.float32) * result_round.astype(jnp.float32),
        axis=-1,
        keepdims=True,
    )
    dprob_anc = jnp.einsum(
        "bmd,ad->bma", gradient_row_set, value_anc, preferred_element_type=jnp.float32
    )
    own_probability_grad = jnp.einsum(
        "flh,feh->fle", gradient_row_set, private_values, preferred_element_type=jnp.float32
    )
    dscore_anc = (prob_anc * (dprob_anc - delta_rows)).astype(jnp.bfloat16)
    own_score_grad = (prob_own * (own_probability_grad - delta_rows)).astype(jnp.bfloat16)
    query_portion = (
        jnp.einsum("bma,ad->bmd", dscore_anc, key_anc, preferred_element_type=jnp.float32)
        + jnp.einsum(
            "oiz,ozv->oiv", own_score_grad, private_keys, preferred_element_type=jnp.float32
        )
    ) * logit_scale
    dkey_anc = (
        jnp.einsum("bma,bmd->ad", dscore_anc, query_row_set, preferred_element_type=jnp.float32)
        * logit_scale
    )
    dvalue_anc = jnp.einsum(
        "bma,bmd->ad", round_anc, gradient_row_set, preferred_element_type=jnp.float32
    )
    dkey_own = (
        jnp.einsum(
            "ers,erc->esc", own_score_grad, query_row_set, preferred_element_type=jnp.float32
        )
        * logit_scale
    )
    dvalue_own = jnp.einsum(
        "ers,erc->esc", private_round, gradient_row_set, preferred_element_type=jnp.float32
    )
    return (result_round, query_portion, dkey_anc, dvalue_anc, dkey_own, dvalue_own)


def on_device(
    queries, leaf_keys, leaf_values, inner_keys, inner_values, out_grad, ancestors, depths
):
    seg_count = lax.axis_size("seg")
    leaf_count = lax.axis_size("leaf")
    seg_here = lax.axis_index("seg")
    leaf_here = lax.axis_index("leaf")
    leaf_dev, rows_here, query_width = queries.shape
    slot_count = inner_keys.shape[0]
    key_width = leaf_keys.shape[2]
    kv_heads = key_width // HD
    group_heads = query_width // key_width
    seg_len = rows_here * leaf_count
    levels = ancestors.shape[1]
    group_lists = ancestors[::leaf_dev]
    group_depth = depths[::leaf_dev]
    owners = group_lists // slot_count
    slot_of = group_lists % slot_count
    level_ids = jnp.arange(levels, dtype=jnp.int32)
    alive_levels = level_ids[None, :] < group_depth[:, None]
    served = alive_levels & (owners == seg_here)
    slot_ids = jnp.arange(slot_count, dtype=jnp.int32)
    serve_pick = jnp.sum(
        (served[:, :, None] & (slot_of[:, :, None] == slot_ids[None, None, :])).astype(jnp.float32),
        axis=1,
    ).astype(jnp.bfloat16)
    stored = jnp.concatenate([inner_keys, inner_values], axis=2)
    outgoing = jnp.einsum(
        "gs,src->grc", serve_pick, stored, preferred_element_type=jnp.float32
    ).astype(jnp.bfloat16)
    arrived = lax.all_to_all(outgoing, "seg", split_axis=0, concat_axis=0, tiled=True)
    my_owners = jnp.take(owners, seg_here, axis=0)
    my_alive = jnp.take(alive_levels, seg_here, axis=0)
    ancestor_rows = jnp.where(
        my_alive[:, None, None], jnp.take(arrived, my_owners, axis=0), jnp.zeros((), jnp.bfloat16)
    )
    own_rows = jnp.concatenate([leaf_keys, leaf_values], axis=2)
    anc_visible = jnp.repeat(my_alive, seg_len)
    blocks = jnp.concatenate([ancestor_rows, own_rows], axis=0)
    by_head = head_major(blocks, kv_heads, HD)
    query_heads = queries.reshape(leaf_dev, rows_here, kv_heads, group_heads * HD).transpose(
        2, 0, 1, 3
    )
    grad_heads = out_grad.reshape(leaf_dev, rows_here, kv_heads, group_heads * HD).transpose(
        2, 0, 1, 3
    )
    row_ids = leaf_here * rows_here + jnp.arange(rows_here, dtype=jnp.int32)
    causal = jnp.arange(seg_len, dtype=jnp.int32)[None, :] <= row_ids[:, None]
    own_visible = jnp.repeat(causal, group_heads, axis=0)

    def head_step(operands):
        query_head, grad_head, packed_head = operands
        whole_rows = lax.all_gather(packed_head, "leaf", axis=1, tiled=True)
        key_anc = whole_rows[:levels, :, :HD].reshape(levels * seg_len, HD)
        value_anc = whole_rows[:levels, :, HD:].reshape(levels * seg_len, HD)
        private_keys = whole_rows[levels:, :, :HD]
        private_values = whole_rows[levels:, :, HD:]
        query_row_set = query_head.reshape(leaf_dev, rows_here * group_heads, HD)
        gradient_row_set = grad_head.reshape(leaf_dev, rows_here * group_heads, HD)
        result_round, query_portion, dkey_anc, dvalue_anc, dkey_own, dvalue_own = attend_block(
            query_row_set,
            gradient_row_set,
            key_anc,
            value_anc,
            private_keys,
            private_values,
            anc_visible,
            own_visible,
        )
        key_grads = jnp.concatenate([dkey_anc.reshape(levels, seg_len, HD), dkey_own], axis=0)
        value_grads = jnp.concatenate([dvalue_anc.reshape(levels, seg_len, HD), dvalue_own], axis=0)
        reduced = lax.psum_scatter(
            jnp.concatenate([key_grads, value_grads], axis=2),
            "leaf",
            scatter_dimension=1,
            tiled=True,
        )
        return (
            result_round.reshape(leaf_dev, rows_here, group_heads * HD),
            query_portion.astype(jnp.bfloat16).reshape(leaf_dev, rows_here, group_heads * HD),
            reduced,
        )

    result_heads, dquery_heads, reduced_heads = lax.map(
        head_step, (query_heads, grad_heads, by_head)
    )
    attention = result_heads.transpose(1, 2, 0, 3).reshape(leaf_dev, rows_here, query_width)
    query_grad = dquery_heads.transpose(1, 2, 0, 3).reshape(leaf_dev, rows_here, query_width)
    summed = column_major(reduced_heads, kv_heads, HD)
    anc_part = summed[:levels]
    own_grads = summed[levels:].astype(jnp.bfloat16)
    leaf_key_grad = own_grads[:, :, :key_width]
    leaf_value_grad = own_grads[:, :, key_width:]
    part_round = anc_part.astype(jnp.bfloat16)
    seg_ids = jnp.arange(seg_count, dtype=jnp.int32)
    homeward_pick = ((my_owners[None, :] == seg_ids[:, None]) & my_alive[None, :]).astype(
        jnp.bfloat16
    )
    homeward = jnp.einsum(
        "ok,krc->orc", homeward_pick, part_round, preferred_element_type=jnp.float32
    ).astype(jnp.bfloat16)
    returned = lax.all_to_all(homeward, "seg", split_axis=0, concat_axis=0, tiled=True)
    collected = jnp.einsum(
        "gs,grc->src", serve_pick, returned, preferred_element_type=jnp.float32
    ).astype(jnp.bfloat16)
    return (
        attention,
        query_grad,
        leaf_key_grad,
        leaf_value_grad,
        collected[:, :, :key_width],
        collected[:, :, key_width:],
    )


def solution(mesh):
    return jax.shard_map(
        on_device,
        mesh=mesh,
        in_specs=(
            P("seg", "leaf", None),
            P("seg", "leaf", None),
            P("seg", "leaf", None),
            P("seg", "leaf", None),
            P("seg", "leaf", None),
            P("seg", "leaf", None),
            P(),
            P(),
        ),
        out_specs=(
            P("seg", "leaf", None),
            P("seg", "leaf", None),
            P("seg", "leaf", None),
            P("seg", "leaf", None),
            P("seg", "leaf", None),
            P("seg", "leaf", None),
        ),
        check_vma=False,
    )
```

profile of v0, /device:TPU:1, one launch (start us, length us, event | category | flops | bytes accessed | tf_op | source)
XLA Modules:
  0.0 1323.1 jit_solution(9653723527980471428)
XLA Ops:
  13.4 5.8 all-to-all-start
  25.5 8.7 all-to-all-done
  39.1 1248.2 %while.17 = (s32[]{:T(128)}, bf16[8,4,32,640]{3,2,1,0:T(8,128)(2,1)}, bf16[8,4,32,640]{3,2,1,0:T(8,128)(2,1)}, bf16[8,8,32,256]{3,1,2,0:T(8,128)(2,1)}, bf16[8,4...) while((s32[]{:T(128)}, ...), condition=%wide.region_8.9_spmd.clone, body=%wide.region_1.8_spmd.clone.sunk | while | flops 2550151168 | bytes 133755288 | solution.py:183
  43.9 43.0 %all-gather.6.cloned.1.call-done = bf16[1,8,512,256]{3,2,1,0:T(8,128)(2,1)} async-done(((bf16[1,8,32,256]{3,2,1,0:T(8,128)(2,1)}), bf16[1,8,512,256]{3,2,1,0:T(8,128)(2,1)}) %all-gather.6.cloned.1.call-update) | async-done | bytes 2097168 | tf_op jit(solution)/shard_map/while/body/eval_jaxpr/all_gather | solution.py:152
  110.3 5.5 copy.107
  120.9 72.7 %reduce-scatter.2.cloned.1.call-done = f32[8,32,256]{2,0,1:T(8,128)} async-done(((f32[8,512,256]{2,0,1:T(8,128)}), f32[8,32,256]{2,0,1:T(8,128)}) %reduce-scatter.2.cloned.1.call-update) | async-done | bytes 262160 | tf_op jit(solution)/shard_map/while/body/eval_jaxpr/reduce_scatter | solution.py:171
  200.0 43.1 %all-gather.6.cloned.1.call-done = bf16[1,8,512,256]{3,2,1,0:T(8,128)(2,1)} async-done(((bf16[1,8,32,256]{3,2,1,0:T(8,128)(2,1)}), bf16[1,8,512,256]{3,2,1,0:T(8,128)(2,1)}) %all-gather.6.cloned.1.call-update) | async-done | bytes 2097168 | tf_op jit(solution)/shard_map/while/body/eval_jaxpr/all_gather | solution.py:152
  266.4 5.5 copy.107
  277.0 72.7 %reduce-scatter.2.cloned.1.call-done = f32[8,32,256]{2,0,1:T(8,128)} async-done(((f32[8,512,256]{2,0,1:T(8,128)}), f32[8,32,256]{2,0,1:T(8,128)}) %reduce-scatter.2.cloned.1.call-update) | async-done | bytes 262160 | tf_op jit(solution)/shard_map/while/body/eval_jaxpr/reduce_scatter | solution.py:171
  356.1 42.8 %all-gather.6.cloned.1.call-done = bf16[1,8,512,256]{3,2,1,0:T(8,128)(2,1)} async-done(((bf16[1,8,32,256]{3,2,1,0:T(8,128)(2,1)}), bf16[1,8,512,256]{3,2,1,0:T(8,128)(2,1)}) %all-gather.6.cloned.1.call-update) | async-done | bytes 2097168 | tf_op jit(solution)/shard_map/while/body/eval_jaxpr/all_gather | solution.py:152
  422.2 5.5 copy.107
  432.8 72.6 %reduce-scatter.2.cloned.1.call-done = f32[8,32,256]{2,0,1:T(8,128)} async-done(((f32[8,512,256]{2,0,1:T(8,128)}), f32[8,32,256]{2,0,1:T(8,128)}) %reduce-scatter.2.cloned.1.call-update) | async-done | bytes 262160 | tf_op jit(solution)/shard_map/while/body/eval_jaxpr/reduce_scatter | solution.py:171
  511.8 43.1 %all-gather.6.cloned.1.call-done = bf16[1,8,512,256]{3,2,1,0:T(8,128)(2,1)} async-done(((bf16[1,8,32,256]{3,2,1,0:T(8,128)(2,1)}), bf16[1,8,512,256]{3,2,1,0:T(8,128)(2,1)}) %all-gather.6.cloned.1.call-update) | async-done | bytes 2097168 | tf_op jit(solution)/shard_map/while/body/eval_jaxpr/all_gather | solution.py:152
  588.8 72.7 %reduce-scatter.2.cloned.1.call-done = f32[8,32,256]{2,0,1:T(8,128)} async-done(((f32[8,512,256]{2,0,1:T(8,128)}), f32[8,32,256]{2,0,1:T(8,128)}) %reduce-scatter.2.cloned.1.call-update) | async-done | bytes 262160 | tf_op jit(solution)/shard_map/while/body/eval_jaxpr/reduce_scatter | solution.py:171
  668.0 43.1 %all-gather.6.cloned.1.call-done = bf16[1,8,512,256]{3,2,1,0:T(8,128)(2,1)} async-done(((bf16[1,8,32,256]{3,2,1,0:T(8,128)(2,1)}), bf16[1,8,512,256]{3,2,1,0:T(8,128)(2,1)}) %all-gather.6.cloned.1.call-update) | async-done | bytes 2097168 | tf_op jit(solution)/shard_map/while/body/eval_jaxpr/all_gather | solution.py:152
  745.0 72.7 %reduce-scatter.2.cloned.1.call-done = f32[8,32,256]{2,0,1:T(8,128)} async-done(((f32[8,512,256]{2,0,1:T(8,128)}), f32[8,32,256]{2,0,1:T(8,128)}) %reduce-scatter.2.cloned.1.call-update) | async-done | bytes 262160 | tf_op jit(solution)/shard_map/while/body/eval_jaxpr/reduce_scatter | solution.py:171
  824.1 43.1 %all-gather.6.cloned.1.call-done = bf16[1,8,512,256]{3,2,1,0:T(8,128)(2,1)} async-done(((bf16[1,8,32,256]{3,2,1,0:T(8,128)(2,1)}), bf16[1,8,512,256]{3,2,1,0:T(8,128)(2,1)}) %all-gather.6.cloned.1.call-update) | async-done | bytes 2097168 | tf_op jit(solution)/shard_map/while/body/eval_jaxpr/all_gather | solution.py:152
  901.1 72.7 %reduce-scatter.2.cloned.1.call-done = f32[8,32,256]{2,0,1:T(8,128)} async-done(((f32[8,512,256]{2,0,1:T(8,128)}), f32[8,32,256]{2,0,1:T(8,128)}) %reduce-scatter.2.cloned.1.call-update) | async-done | bytes 262160 | tf_op jit(solution)/shard_map/while/body/eval_jaxpr/reduce_scatter | solution.py:171
  980.2 43.1 %all-gather.6.cloned.1.call-done = bf16[1,8,512,256]{3,2,1,0:T(8,128)(2,1)} async-done(((bf16[1,8,32,256]{3,2,1,0:T(8,128)(2,1)}), bf16[1,8,512,256]{3,2,1,0:T(8,128)(2,1)}) %all-gather.6.cloned.1.call-update) | async-done | bytes 2097168 | tf_op jit(solution)/shard_map/while/body/eval_jaxpr/all_gather | solution.py:152
  1057.2 72.6 %reduce-scatter.2.cloned.1.call-done = f32[8,32,256]{2,0,1:T(8,128)} async-done(((f32[8,512,256]{2,0,1:T(8,128)}), f32[8,32,256]{2,0,1:T(8,128)}) %reduce-scatter.2.cloned.1.call-update) | async-done | bytes 262160 | tf_op jit(solution)/shard_map/while/body/eval_jaxpr/reduce_scatter | solution.py:171
  1136.3 42.8 %all-gather.6.cloned.1.call-done = bf16[1,8,512,256]{3,2,1,0:T(8,128)(2,1)} async-done(((bf16[1,8,32,256]{3,2,1,0:T(8,128)(2,1)}), bf16[1,8,512,256]{3,2,1,0:T(8,128)(2,1)}) %all-gather.6.cloned.1.call-update) | async-done | bytes 2097168 | tf_op jit(solution)/shard_map/while/body/eval_jaxpr/all_gather | solution.py:152
  1213.0 72.7 %reduce-scatter.2.cloned.1.call-done = f32[8,32,256]{2,0,1:T(8,128)} async-done(((f32[8,512,256]{2,0,1:T(8,128)}), f32[8,32,256]{2,0,1:T(8,128)}) %reduce-scatter.2.cloned.1.call-update) | async-done | bytes 262160 | tf_op jit(solution)/shard_map/while/body/eval_jaxpr/reduce_scatter | solution.py:171
  1292.5 6.7 all-to-all-start.1
  1303.6 10.6 all-to-all-done.1
  (499 shorter events, 333.9 us)
Async XLA Ops:
  11.8 7.4 copy-start.8
  13.4 20.9 %all-to-all-start = ((bf16[8,32,2048]{2,1,0:T(8,128)(2,1)}), bf16[8,32,2048]{2,1,0:T(8,128)(2,1)}, u32[]{:S(2)}, u32[]{:S(2)}) async-start(bf16[8,32,2048]{2,1,0:T(8,128)(2,1)} %copy.66), calls=%async_computation.1 | async-start | bytes 2097152 | tf_op jit(solution)/shard_map/all_to_all | solution.py:130
  25.0 11.3 copy-start.7
  25.2 11.2 copy-start.14
  39.1 47.9 %all-gather.6.cloned.1.call-start = ((), (), s32[]{:S(2)}) async-start(), calls=%async_computation.3 | async-start | bytes 2228224 | tf_op jit(solution)/shard_map/while/body/eval_jaxpr/all_gather | solution.py:152
  40.7 152.9 %reduce-scatter.2.cloned.1.call-start = ((), (), s32[]{:S(2)}) async-start(), calls=%async_computation.4 | async-start | bytes 4456448 | tf_op jit(solution)/shard_map/while/body/eval_jaxpr/reduce_scatter | solution.py:171
  115.8 4.2 copy-start.5
  195.2 47.9 %all-gather.6.cloned.1.call-start = ((), (), s32[]{:S(2)}) async-start(), calls=%async_computation.3 | async-start | bytes 2228224 | tf_op jit(solution)/shard_map/while/body/eval_jaxpr/all_gather | solution.py:152
  196.7 152.9 %reduce-scatter.2.cloned.1.call-start = ((), (), s32[]{:S(2)}) async-start(), calls=%async_computation.4 | async-start | bytes 4456448 | tf_op jit(solution)/shard_map/while/body/eval_jaxpr/reduce_scatter | solution.py:171
  271.9 4.2 copy-start.5
  351.3 47.6 %all-gather.6.cloned.1.call-start = ((), (), s32[]{:S(2)}) async-start(), calls=%async_computation.3 | async-start | bytes 2228224 | tf_op jit(solution)/shard_map/while/body/eval_jaxpr/all_gather | solution.py:152
  352.9 152.5 %reduce-scatter.2.cloned.1.call-start = ((), (), s32[]{:S(2)}) async-start(), calls=%async_computation.4 | async-start | bytes 4456448 | tf_op jit(solution)/shard_map/while/body/eval_jaxpr/reduce_scatter | solution.py:171
  507.0 47.9 %all-gather.6.cloned.1.call-start = ((), (), s32[]{:S(2)}) async-start(), calls=%async_computation.3 | async-start | bytes 2228224 | tf_op jit(solution)/shard_map/while/body/eval_jaxpr/all_gather | solution.py:152
  508.6 152.9 %reduce-scatter.2.cloned.1.call-start = ((), (), s32[]{:S(2)}) async-start(), calls=%async_computation.4 | async-start | bytes 4456448 | tf_op jit(solution)/shard_map/while/body/eval_jaxpr/reduce_scatter | solution.py:171
  663.1 47.9 %all-gather.6.cloned.1.call-start = ((), (), s32[]{:S(2)}) async-start(), calls=%async_computation.3 | async-start | bytes 2228224 | tf_op jit(solution)/shard_map/while/body/eval_jaxpr/all_gather | solution.py:152
  664.7 152.9 %reduce-scatter.2.cloned.1.call-start = ((), (), s32[]{:S(2)}) async-start(), calls=%async_computation.4 | async-start | bytes 4456448 | tf_op jit(solution)/shard_map/while/body/eval_jaxpr/reduce_scatter | solution.py:171
  819.3 47.9 %all-gather.6.cloned.1.call-start = ((), (), s32[]{:S(2)}) async-start(), calls=%async_computation.3 | async-start | bytes 2228224 | tf_op jit(solution)/shard_map/while/body/eval_jaxpr/all_gather | solution.py:152
  820.9 152.9 %reduce-scatter.2.cloned.1.call-start = ((), (), s32[]{:S(2)}) async-start(), calls=%async_computation.4 | async-start | bytes 4456448 | tf_op jit(solution)/shard_map/while/body/eval_jaxpr/reduce_scatter | solution.py:171
  975.4 47.9 %all-gather.6.cloned.1.call-start = ((), (), s32[]{:S(2)}) async-start(), calls=%async_computation.3 | async-start | bytes 2228224 | tf_op jit(solution)/shard_map/while/body/eval_jaxpr/all_gather | solution.py:152
  977.0 152.8 %reduce-scatter.2.cloned.1.call-start = ((), (), s32[]{:S(2)}) async-start(), calls=%async_computation.4 | async-start | bytes 4456448 | tf_op jit(solution)/shard_map/while/body/eval_jaxpr/reduce_scatter | solution.py:171
  1131.4 47.6 %all-gather.6.cloned.1.call-start = ((), (), s32[]{:S(2)}) async-start(), calls=%async_computation.3 | async-start | bytes 2228224 | tf_op jit(solution)/shard_map/while/body/eval_jaxpr/all_gather | solution.py:152
  1133.0 152.6 %reduce-scatter.2.cloned.1.call-start = ((), (), s32[]{:S(2)}) async-start(), calls=%async_computation.4 | async-start | bytes 4456448 | tf_op jit(solution)/shard_map/while/body/eval_jaxpr/reduce_scatter | solution.py:171
  1292.5 21.7 %all-to-all-start.1 = ((bf16[8,32,2048]{2,1,0:T(8,128)(2,1)}), bf16[8,32,2048]{2,1,0:T(8,128)(2,1)S(1)}, u32[]{:S(2)}, u32[]{:S(2)}) async-start(bf16[8,32,2048]{2,1,0:T(8,128)(2,1)} %copy.74), calls=%async_computation.2 | async-start | bytes 2097152 | tf_op jit(solution)/shard_map/all_to_all | solution.py:201
  1301.1 13.1 copy-start.17
  (61 other events, 149.0 us)
Sparse Core Ops, SparseCore 0:
  42.6 44.3 all-gather.5
  115.9 77.5 reduce-scatter.1
  198.7 44.3 all-gather.5
  272.0 77.5 reduce-scatter.1
  354.5 44.3 all-gather.5
  427.8 77.5 reduce-scatter.1
  510.5 44.3 all-gather.5
  583.9 77.6 reduce-scatter.1
  666.6 44.3 all-gather.5
  740.0 77.6 reduce-scatter.1
  822.8 44.3 all-gather.5
  896.1 77.6 reduce-scatter.1
  978.9 44.3 all-gather.5
  1052.2 77.5 reduce-scatter.1
  1134.7 44.3 all-gather.5
  1208.0 77.5 reduce-scatter.1
where the time goes:
time: 1330 us; the launch traced here: 1320 us
  waiting for transfers between devices  945 us (71%)
  local copies, waits for them, and re-layouts  172 us (13%)
  matrix products  130 us (10%)
  other arithmetic  47.1 us (4%)
  between operations  14 us (1%)
    reduce_scatter x8, waiting for transfers between devices, head_step(): lax.psum_scatter(jnp.concatenate([key_grads, value_grads], axis=2), 'leaf...  581 us
    all_gather x8, waiting for transfers between devices, head_step(): whole_rows = lax.all_gather(packed_head, 'leaf', axis=1, tiled=True)  344 us
    concatenate x8, local copies, waits for them, and re-layouts, head_step(): jnp.concatenate([key_grads, value_grads], axis=2)  43.7 us
    dynamic_slice x24, local copies, waits for them, and re-layouts, on_device(): lax.map(head_step, (query_heads, grad_heads, by_head))  27.5 us
  transfers between devices with their start and end apart: 18, of which 18 were waited for; matrix products, arithmetic and copies ran while one was open for 6% of the time, Pallas kernels for 0%

commit v1 on v0

--- a/solution.py
+++ b/solution.py
@@ -6,6 +6,29 @@
 
 HD = 128
 NEG_FILL = -1e30
+
+
+def group_samples(k_dim, link_axis, a0):
+    z = lax.psum(1, link_axis)
+    mid_arr = lax.axis_index(link_axis)
+    front, h_now, local_next = (z, mid_arr, a0.shape[k_dim])
+    queue = [(u, (u + 1) % front) for u in range(front)]
+    fields = [(u, (u - 1) % front) for u in range(front)]
+    high = jnp.zeros((*a0.shape[:k_dim], front * local_next, *a0.shape[k_dim + 1 :]), a0.dtype)
+    q_next = frame_out = a0
+    high = lax.dynamic_update_slice_in_dim(high, a0, h_now * local_next, axis=k_dim)
+    outer = front // 2
+    for hop_no in tuple(range(1, outer + 1)):
+        q_next = lax.ppermute(q_next, link_axis, queue)
+        high = lax.dynamic_update_slice_in_dim(
+            high, q_next, (h_now - hop_no) % front * local_next, axis=k_dim
+        )
+        if hop_no < front - outer:
+            frame_out = lax.ppermute(frame_out, link_axis, fields)
+            high = lax.dynamic_update_slice_in_dim(
+                high, frame_out, (h_now + hop_no) % front * local_next, axis=k_dim
+            )
+    return high
 
 
 def head_major(packed, kv_heads, head_size):
@@ -149,7 +172,7 @@
 
     def head_step(operands):
         query_head, grad_head, packed_head = operands
-        whole_rows = lax.all_gather(packed_head, "leaf", axis=1, tiled=True)
+        whole_rows = group_samples(1, "leaf", packed_head)
         key_anc = whole_rows[:levels, :, :HD].reshape(levels * seg_len, HD)
         value_anc = whole_rows[:levels, :, HD:].reshape(levels * seg_len, HD)
         private_keys = whole_rows[levels:, :, :HD]

time: 1330 us -> 1470 us (1.11)
  starting transfers between devices: 12.9 us -> 290 us
  waiting for transfers between devices: 945 us -> 828 us
  local copies, waits for them, and re-layouts: 172 us -> 149 us
    all_gather x8 -> x0, waiting for transfers between devices: 344 us -> none  [head_step(): whole_rows = lax.all_gather(packed_head, 'leaf', axis=1, tiled=True)]
    ppermute x0 -> x120, starting transfers between devices: none -> 277 us  [the longest x56 271 us: group_samples(): frame_out = lax.ppermute(frame_out, link_axis, fields)]
    ppermute x0 -> x120, waiting for transfers between devices: none -> 178 us  [the longest x64 177 us: group_samples(): q_next = lax.ppermute(q_next, link_axis, queue)]
    reduce_scatter x8, waiting for transfers between devices: 581 us -> 631 us  [head_step(): lax.psum_scatter(jnp.concatenate([key_grads, value_grads], axis=2), 'leaf...]
    dot_general x8, matrix products: 4.97 us -> 20.1 us  [attend_block(): jnp.einsum('bma,bmd->ad', round_anc, gradient_row_set, preferred_element_...]
  transfers between devices with their start and end apart: 18 -> 130, of which waited for: 18 -> 67; matrix products, arithmetic and copies ran while one was open for 6% -> 5% of each run, Pallas kernels for 0% -> 0%
where the time goes in v1:
time: 1470 us
  waiting for transfers between devices  828 us (56%)
  starting transfers between devices  290 us (20%)
  local copies, waits for them, and re-layouts  149 us (10%)
  matrix products  138 us (9%)
  other arithmetic  47.5 us (3%)
    reduce_scatter x8, waiting for transfers between devices, head_step(): lax.psum_scatter(jnp.concatenate([key_grads, value_grads], axis=2), 'leaf...  631 us
    ppermute x56, starting transfers between devices, group_samples(): frame_out = lax.ppermute(frame_out, link_axis, fields)  271 us
    ppermute x64, waiting for transfers between devices, group_samples(): q_next = lax.ppermute(q_next, link_axis, queue)  177 us
    concatenate x8, local copies, waits for them, and re-layouts, head_step(): jnp.concatenate([key_grads, value_grads], axis=2)  43.4 us
  transfers between devices with their start and end apart: 130, of which 67 were waited for; matrix products, arithmetic and copies ran while one was open for 5% of the time, Pallas kernels for 0%

profile of v1, /device:TPU:1, one launch (start us, length us, event | category | flops | bytes accessed | tf_op | source)
XLA Modules:
  0.0 1471.8 jit_solution(5021965165384656302)
XLA Ops:
  12.9 5.8 all-to-all-start
  24.3 9.5 all-to-all-done
  38.7 1397.0 %while.19 = (s32[]{:T(128)}, bf16[8,4,32,640]{3,2,1,0:T(8,128)(2,1)}, bf16[8,4,32,640]{3,2,1,0:T(8,128)(2,1)}, bf16[8,8,32,256]{3,1,2,0:T(8,128)(2,1)}, bf16[8,4...) while((s32[]{:T(128)}, ...), condition=%wide.region_8.9_spmd.clone, body=%wide.region_1.8_spmd.clone.sunk | while | flops 2550151680 | bytes 146079504 | solution.py:206
  93.2 8.5 collective-permute-done.14
  134.0 75.7 %reduce-scatter.2.cloned.1.call-done = f32[8,32,256]{2,0,1:T(8,128)} async-done(((f32[8,512,256]{2,0,1:T(8,128)}), f32[8,32,256]{2,0,1:T(8,128)}) %reduce-scatter.2.cloned.1.call-update) | async-done | bytes 262160 | tf_op jit(solution)/shard_map/while/body/eval_jaxpr/reduce_scatter | solution.py:194
  257.9 5.5 collective-permute-start.13
  265.9 7.1 collective-permute-done.14
  305.4 79.3 %reduce-scatter.2.cloned.1.call-done = f32[8,32,256]{2,0,1:T(8,128)} async-done(((f32[8,512,256]{2,0,1:T(8,128)}), f32[8,32,256]{2,0,1:T(8,128)}) %reduce-scatter.2.cloned.1.call-update) | async-done | bytes 262160 | tf_op jit(solution)/shard_map/while/body/eval_jaxpr/reduce_scatter | solution.py:194
  440.9 7.1 collective-permute-done.14
  480.4 79.3 %reduce-scatter.2.cloned.1.call-done = f32[8,32,256]{2,0,1:T(8,128)} async-done(((f32[8,512,256]{2,0,1:T(8,128)}), f32[8,32,256]{2,0,1:T(8,128)}) %reduce-scatter.2.cloned.1.call-update) | async-done | bytes 262160 | tf_op jit(solution)/shard_map/while/body/eval_jaxpr/reduce_scatter | solution.py:194
  607.8 5.5 collective-permute-start.13
  615.8 7.1 collective-permute-done.14
  655.2 79.3 %reduce-scatter.2.cloned.1.call-done = f32[8,32,256]{2,0,1:T(8,128)} async-done(((f32[8,512,256]{2,0,1:T(8,128)}), f32[8,32,256]{2,0,1:T(8,128)}) %reduce-scatter.2.cloned.1.call-update) | async-done | bytes 262160 | tf_op jit(solution)/shard_map/while/body/eval_jaxpr/reduce_scatter | solution.py:194
  790.7 7.1 collective-permute-done.14
  830.1 79.3 %reduce-scatter.2.cloned.1.call-done = f32[8,32,256]{2,0,1:T(8,128)} async-done(((f32[8,512,256]{2,0,1:T(8,128)}), f32[8,32,256]{2,0,1:T(8,128)}) %reduce-scatter.2.cloned.1.call-update) | async-done | bytes 262160 | tf_op jit(solution)/shard_map/while/body/eval_jaxpr/reduce_scatter | solution.py:194
  965.6 7.1 collective-permute-done.14
  1005.1 79.2 %reduce-scatter.2.cloned.1.call-done = f32[8,32,256]{2,0,1:T(8,128)} async-done(((f32[8,512,256]{2,0,1:T(8,128)}), f32[8,32,256]{2,0,1:T(8,128)}) %reduce-scatter.2.cloned.1.call-update) | async-done | bytes 262160 | tf_op jit(solution)/shard_map/while/body/eval_jaxpr/reduce_scatter | solution.py:194
  1140.4 7.1 collective-permute-done.14
  1179.9 79.3 %reduce-scatter.2.cloned.1.call-done = f32[8,32,256]{2,0,1:T(8,128)} async-done(((f32[8,512,256]{2,0,1:T(8,128)}), f32[8,32,256]{2,0,1:T(8,128)}) %reduce-scatter.2.cloned.1.call-update) | async-done | bytes 262160 | tf_op jit(solution)/shard_map/while/body/eval_jaxpr/reduce_scatter | solution.py:194
  1307.3 5.5 collective-permute-start.13
  1315.3 7.1 collective-permute-done.14
  1354.8 79.2 %reduce-scatter.2.cloned.1.call-done = f32[8,32,256]{2,0,1:T(8,128)} async-done(((f32[8,512,256]{2,0,1:T(8,128)}), f32[8,32,256]{2,0,1:T(8,128)}) %reduce-scatter.2.cloned.1.call-update) | async-done | bytes 262160 | tf_op jit(solution)/shard_map/while/body/eval_jaxpr/reduce_scatter | solution.py:194
  1440.9 6.7 all-to-all-start.1
  1452.5 10.0 all-to-all-done.1
  (873 shorter events, 715.0 us)
Async XLA Ops:
  12.9 20.9 %all-to-all-start = ((bf16[8,32,2048]{2,1,0:T(8,128)(2,1)}), bf16[8,32,2048]{2,1,0:T(8,128)(2,1)}, u32[]{:S(2)}, u32[]{:S(2)}) async-start(bf16[8,32,2048]{2,1,0:T(8,128)(2,1)} %copy.66), calls=%async_computation.1 | async-start | bytes 2097152 | tf_op jit(solution)/shard_map/all_to_all | solution.py:153
  38.7 171.1 %reduce-scatter.2.cloned.1.call-start = ((), (), s32[]{:S(2)}) async-start(), calls=%async_computation.3 | async-start | bytes 4456448 | tf_op jit(solution)/shard_map/while/body/eval_jaxpr/reduce_scatter | solution.py:194
  39.7 9.9 collective-permute-start
  41.1 8.6 collective-permute-start.1
  93.1 8.5 collective-permute-start.14
  211.4 173.3 %reduce-scatter.2.cloned.1.call-start = ((), (), s32[]{:S(2)}) async-start(), calls=%async_computation.3 | async-start | bytes 4456448 | tf_op jit(solution)/shard_map/while/body/eval_jaxpr/reduce_scatter | solution.py:194
  212.5 8.4 collective-permute-start
  386.3 173.4 %reduce-scatter.2.cloned.1.call-start = ((), (), s32[]{:S(2)}) async-start(), calls=%async_computation.3 | async-start | bytes 4456448 | tf_op jit(solution)/shard_map/while/body/eval_jaxpr/reduce_scatter | solution.py:194
  424.5 8.4 collective-permute-start.10
  424.5 8.4 collective-permute-start.11
  561.3 173.2 %reduce-scatter.2.cloned.1.call-start = ((), (), s32[]{:S(2)}) async-start(), calls=%async_computation.3 | async-start | bytes 4456448 | tf_op jit(solution)/shard_map/while/body/eval_jaxpr/reduce_scatter | solution.py:194
  562.4 8.4 collective-permute-start
  736.1 173.3 %reduce-scatter.2.cloned.1.call-start = ((), (), s32[]{:S(2)}) async-start(), calls=%async_computation.3 | async-start | bytes 4456448 | tf_op jit(solution)/shard_map/while/body/eval_jaxpr/reduce_scatter | solution.py:194
  774.2 8.4 collective-permute-start.10
  774.2 8.4 collective-permute-start.11
  911.0 173.2 %reduce-scatter.2.cloned.1.call-start = ((), (), s32[]{:S(2)}) async-start(), calls=%async_computation.3 | async-start | bytes 4456448 | tf_op jit(solution)/shard_map/while/body/eval_jaxpr/reduce_scatter | solution.py:194
  912.1 8.4 collective-permute-start
  949.2 8.4 collective-permute-start.10
  949.2 8.4 collective-permute-start.11
  1085.9 173.3 %reduce-scatter.2.cloned.1.call-start = ((), (), s32[]{:S(2)}) async-start(), calls=%async_computation.3 | async-start | bytes 4456448 | tf_op jit(solution)/shard_map/while/body/eval_jaxpr/reduce_scatter | solution.py:194
  1124.0 8.4 collective-permute-start.10
  1124.0 8.4 collective-permute-start.11
  1260.8 173.2 %reduce-scatter.2.cloned.1.call-start = ((), (), s32[]{:S(2)}) async-start(), calls=%async_computation.3 | async-start | bytes 4456448 | tf_op jit(solution)/shard_map/while/body/eval_jaxpr/reduce_scatter | solution.py:194
  1440.9 21.7 %all-to-all-start.1 = ((bf16[8,32,2048]{2,1,0:T(8,128)(2,1)}), bf16[8,32,2048]{2,1,0:T(8,128)(2,1)S(1)}, u32[]{:S(2)}, u32[]{:S(2)}) async-start(bf16[8,32,2048]{2,1,0:T(8,128)(2,1)} %copy.74), calls=%async_computation.2 | async-start | bytes 2097152 | tf_op jit(solution)/shard_map/all_to_all | solution.py:224
  (188 other events, 1484.0 us)
Sparse Core Ops, SparseCore 0:
  130.1 79.5 reduce-scatter.1
  301.5 83.1 reduce-scatter.1
  476.5 83.1 reduce-scatter.1
  651.3 83.1 reduce-scatter.1
  826.3 83.1 reduce-scatter.1
  1001.2 82.9 reduce-scatter.1
  1176.0 83.1 reduce-scatter.1
  1350.9 83.0 reduce-scatter.1
